TPU v7x, 32 devices: a whole 2x2x4 slice. The times are simulated.
32 devices in a mesh: shard: 2 (over core), tensor: 4 (over y, x), section: 4 (over z).
Axes of the slice: x: 2, y: 2, z: 4, core: 2. Of those that a mesh axis runs over, the one named last changes fastest.
Arguments:
- grad_parts: bfloat16 [2, 2304, 2304], P('shard', ('tensor', 'section')), may hold values from -1.5 to 1.5
- moment: float32 [2304, 2304], P('shard', ('tensor', 'section')), may hold values from -6 to 6
- second: float32 [2304, 2304], P('shard', ('tensor', 'section')), may hold values from 0.05 to 2
- stat_left: float32 [2304, 2304], P('shard', ('tensor', 'section')), may hold values from -0.1 to 12
- basis_left: float32 [2304, 2304], P('shard', ('tensor', 'section')), may hold values from -0.2 to 1.5
Outputs:
- update: float32 [2304, 2304], P('shard', ('tensor', 'section'))
- moment_next: float32 [2304, 2304], P('shard', ('tensor', 'section'))
- second_next: float32 [2304, 2304], P('shard', ('tensor', 'section'))
- stat_next: float32 [2304, 2304], P('shard', ('tensor', 'section'))
- basis_next: float32 [2304, 2304], P('shard', ('tensor', 'section'))
All inputs are finite; a program needn't handle non-finite values.
Results may differ from a plain program's by a relative error of at most 0.00074.
Values may be sent and summed in bfloat16 or wider, within the bound.
No kernel may reach another device: no remote copies, remote signals or barrier semaphores. Data moves between devices by JAX's collectives and lax.ppermute only.
A program may use at most 128 MiB of HBM per device.

v0:
```python
import jax
import jax.numpy as jnp
from jax import lax
from jax.sharding import PartitionSpec as P

D = 2304
NS_ITERS = 2
beta_one = 0.9
beta_two = 0.95
stat_decay = 0.95
adam_eps = 1e-08
first_fix = 1.0 - 0.9**10
second_fix = 1.0 - 0.95**10
shrink = 0.6
norm_eps = 1e-06
TS = ("tensor", "section")
PAD = 8


def exact_dot(left, right):
    return jnp.dot(left, right, precision=lax.Precision.HIGH, preferred_element_type=jnp.float32)


def contract_rows(left, right):
    return lax.dot_general(
        left,
        right,
        (((0,), (0,)), ((), ())),
        precision=lax.Precision.HIGH,
        preferred_element_type=jnp.float32,
    )


def split_bf16(x):
    top = lax.reduce_precision(x, exponent_bits=8, mantissa_bits=7)
    return (top.astype(jnp.bfloat16), (x - top).astype(jnp.bfloat16))


def bf16_dot(left, right, dims):
    return lax.dot_general(left, right, (dims, ((), ())), preferred_element_type=jnp.float32)


def split_dot(left_hi, left_lo, right, dims):
    right_hi, right_lo = split_bf16(right)
    return (
        bf16_dot(left_hi, right_hi, dims)
        + bf16_dot(left_hi, right_lo, dims)
        + bf16_dot(left_lo, right_hi, dims)
    )


def make_shards(n_shard, n_section, n_ts):
    rows = D // n_shard
    cols = D // n_ts
    assert rows % cols == 0 or cols % rows == 0
    pair = n_shard == 2

    def partner(x):
        return lax.ppermute(x, "shard", [(0, 1), (1, 0)])

    def shard_concat(x, c):
        if not pair:
            return lax.all_gather(x, "shard", axis=0, tiled=True)
        other = partner(x)
        first = jnp.where(c == 0, x, other)
        last = jnp.where(c == 0, other, x)
        return jnp.concatenate([first, last], axis=0)

    def shard_sum(x):
        if not pair:
            return lax.psum(x, "shard")
        return x + partner(x)

    def shard_sum_scatter(x, c, axis):
        if not pair:
            return lax.psum_scatter(x, "shard", scatter_dimension=axis, tiled=True)
        size = x.shape[axis] // 2
        mine = lax.dynamic_slice_in_dim(x, c * size, size, axis=axis)
        theirs = lax.dynamic_slice_in_dim(x, (1 - c) * size, size, axis=axis)
        return mine + partner(theirs)

    def block_rows(grad_rows, k, c):
        start = k * cols
        if cols <= rows:
            piece = lax.dynamic_slice_in_dim(grad_rows, start % rows, cols, axis=0)
            owner = start // rows
            if pair:
                return jnp.where(owner == c, piece, partner(piece))
            pieces = lax.all_gather(piece, "shard", axis=0, tiled=False)
            return lax.dynamic_index_in_dim(pieces, owner, axis=0, keepdims=False)
        full = lax.all_gather(grad_rows, "shard", axis=0, tiled=True)
        return lax.dynamic_slice_in_dim(full, start, cols, axis=0)

    def all_sum(value):
        x = jnp.full((PAD, 128), value, jnp.float32)
        if n_ts & n_ts - 1 == 0:
            step = 1
            while step < n_ts:
                x = x + lax.ppermute(x, TS, [(i, i ^ step) for i in range(n_ts)])
                step *= 2
        else:
            x = lax.psum(x, TS)
        return shard_sum(x)[0, 0]

    def newton_step(iterate):
        iterate_rows = lax.all_gather(iterate, TS, axis=1, tiled=True)
        z_cols = shard_sum(contract_rows(iterate_rows, iterate))
        return 1.5 * iterate - 0.5 * exact_dot(iterate_rows, z_cols)

    def shards(grad_parts, moment, second, stat_left, basis_left):
        c = lax.axis_index("shard")
        k = lax.axis_index("tensor") * n_section + lax.axis_index("section")
        part = grad_parts[0]
        if pair:
            mine = lax.dynamic_slice_in_dim(part, c * rows, rows, axis=1)
            theirs = lax.dynamic_slice_in_dim(part, (1 - c) * rows, rows, axis=1)
            grad_flip = (mine.astype(jnp.float32) + partner(theirs).astype(jnp.float32)).astype(
                jnp.bfloat16
            )
        else:
            grad_flip = lax.psum_scatter(
                part.astype(jnp.float32).astype(jnp.bfloat16),
                "shard",
                scatter_dimension=1,
                tiled=True,
            )
        grad = grad_flip.T
        grad_cols = shard_concat(grad, c)
        basis_hi, basis_lo = split_bf16(basis_left)
        stacked = lax.all_gather(jnp.stack([grad, basis_hi, basis_lo]), TS, axis=2, tiled=True)
        grad_rows, hi_rows, lo_rows = (stacked[0], stacked[1], stacked[2])
        if cols <= rows and pair:
            piece = lax.dynamic_slice(stacked, (0, k * cols % rows, 0), (1, cols, D))[0]
            grad_krows = jnp.where(k * cols // rows == c, piece, partner(piece))
        else:
            grad_krows = block_rows(grad_rows, k, c)
        gram = lax.dot_general(
            grad_rows, grad_krows, (((1,), (1,)), ((), ())), preferred_element_type=jnp.float32
        )
        stat_next = stat_decay * stat_left + (1.0 - stat_decay) / D * gram
        by_rows = ((1,), (0,))
        stat_hi, stat_lo = split_bf16(shard_concat(stat_next, c))
        quads = bf16_dot(stacked[1:], jnp.concatenate([stat_hi, stat_lo], axis=1), ((2,), (0,)))
        power = quads[0, :, :cols] + quads[0, :, cols:] + quads[1, :, :cols]
        power, stacked_later = lax.optimization_barrier((power, stacked))
        hi_later, lo_later = (stacked_later[1], stacked_later[2])
        rotated = bf16_dot(hi_later, grad_cols, by_rows) + bf16_dot(lo_later, grad_cols, by_rows)
        moment_next = beta_one * moment + (1.0 - beta_one) * rotated
        second_next = beta_two * second + (1.0 - beta_two) * rotated * rotated
        ratio = moment_next / first_fix / (jnp.sqrt(second_next / second_fix) + adam_eps)
        update = shard_sum_scatter(split_dot(hi_later, lo_later, ratio, ((0,), (0,))), c, 0)
        power_rows = lax.all_gather(power, TS, axis=1, tiled=True)
        total_sq = all_sum(jnp.sum(power * power))
        power_rows, update, total_sq = lax.optimization_barrier((power_rows, update, total_sq))
        z_cols = shard_sum(contract_rows(power_rows, power))
        scale = shrink * jnp.sqrt(D / (total_sq + norm_eps))
        iterate = 1.5 * scale * power - 0.5 * scale * scale * scale * exact_dot(power_rows, z_cols)
        for turn in range(NS_ITERS - 1):
            iterate = newton_step(iterate)
        return (update, moment_next, second_next, stat_next, iterate)

    return shards


def solution(mesh):
    n_shard = mesh.shape["shard"]
    n_section = mesh.shape["section"]
    n_ts = mesh.shape["tensor"] * n_section
    in_specs = (
        P("shard", TS, None),
        P("shard", TS),
        P("shard", TS),
        P("shard", TS),
        P("shard", TS),
    )
    out_specs = (P("shard", TS), P("shard", TS), P("shard", TS), P("shard", TS), P("shard", TS))
    return jax.shard_map(
        make_shards(n_shard, n_section, n_ts),
        mesh=mesh,
        in_specs=in_specs,
        out_specs=out_specs,
        check_vma=False,
    )
```

profile of v0, /device:TPU:0, one launch (start us, length us, event | category | flops | bytes accessed | tf_op | source)
XLA Modules:
  0.0 523.1 jit_solution(11538976663344151876)
XLA Ops:
  12.3 186.3 %all-gather.4.cloned.1.call-done = bf16[3,1152,2304]{1,2,0:T(8,128)(2,1)} async-done(((bf16[3,1152,144]{1,2,0:T(8,128)(2,1)}), bf16[3,1152,2304]{1,2,0:T(8,128)(2,1)}) %all-gather.4.cloned.1.call-update) | async-done | bytes 15925264 | tf_op jit(solution)/shard_map/all_gather | solution.py:130
  198.6 2.0 constant_dynamic-slice_fusion.1
  201.3 2.1 collective-permute-done.1
  203.4 3.6 fusion.28
  207.3 2.0 collective-permute-done.2
  209.5 6.4 %fusion = f32[2,1152,288]{1,2,0:T(8,128)S(1)} fusion(bf16[3,1152,2304]{1,2,0:T(8,128)(2,1)} %all-gather.4.cloned.1.call-done, bf16[2304,144]{0,1:T(8,128)(2,1)S(1)} %get-tuple-element.16, bf16[2304,144]{0,1:T(8,128)(2,1)S(1)} %get-tuple-element.15), kind=kOutput, calls=%fused_computation | convolution fusion | flops 3060301824 | bytes 14598144 | tf_op jit(solution)/shard_map/dot_general | solution.py:40
  217.3 1.5 collective-permute-done.3
  218.9 3.7 fusion.5
  222.6 5.0 multiply_add_fusion
  227.7 5.0 fusion.7
  232.7 2.0 fusion.18
  234.7 2.0 fusion.21
  238.5 3.6 collective-permute-done.5
  244.2 3.2 collective-permute-done.6
  249.5 2.3 collective-permute-done.7
  253.2 2.2 collective-permute-done.8
  258.1 90.8 %all-gather.6.cloned.1.call-done = f32[1152,2304]{0,1:T(8,128)} async-done(((f32[1152,144]{0,1:T(8,128)}), f32[1152,2304]{0,1:T(8,128)}) %all-gather.6.cloned.1.call-update) | async-done | bytes 10616848 | tf_op jit(solution)/shard_map/all_gather | solution.py:152
  348.8 8.4 %fusion.53 = f32[2304,144]{0,1:T(8,128)S(1)} fusion(f32[1152,2304]{0,1:T(8,128)} %all-gather.6.cloned.1.call-done, f32[1152,144]{0,1:T(8,128)S(1)} %copy-done.1), kind=kOutput, calls=%fused_computation.74 | convolution fusion | flops 2293235712 | bytes 12607488 | tf_op jit(solution)/shard_map/dot_general | solution.py:25
  358.0 2.3 collective-permute-done.10
  360.4 8.3 %fusion.29 = f32[1152,144]{0,1:T(8,128)} fusion(f32[1152,2304]{0,1:T(8,128)} %all-gather.6.cloned.1.call-done, f32[2304,144]{0,1:T(8,128)S(1)} %fusion.53, f32[2304,144]{0,1:T(8,128)S(1)} %collective-permute-done.10, f32[1152,144]{0,1:T(8,128)S(1)} %copy-done.1, f32[]{:T(128)S(6)} %mul.108, f32[]{:T(128)S(6)} %mul.103), kind=kOutput, calls=%fused_computation.26 | convolution fusion | flops 2294065152 | bytes 14598152 | tf_op jit(solution)/shard_map/dot_general | solution.py:21
  368.6 131.8 %all-gather.8.cloned.1.call-done = f32[1152,2304]{0,1:T(8,128)} async-done(((f32[1152,144]{0,1:T(8,128)}), f32[1152,2304]{0,1:T(8,128)}) %all-gather.8.cloned.1.call-update) | async-done | bytes 10616848 | tf_op jit(solution)/shard_map/all_gather | solution.py:106
  500.4 8.6 %fusion.54 = f32[2304,144]{0,1:T(8,128)S(1)} fusion(f32[1152,2304]{0,1:T(8,128)} %all-gather.8.cloned.1.call-done, f32[1152,144]{0,1:T(8,128)} %fusion.29), kind=kOutput, calls=%fused_computation.75 | convolution fusion | flops 2293235712 | bytes 12607488 | tf_op jit(solution)/shard_map/dot_general | solution.py:25
  509.2 3.0 collective-permute-done.11
  512.2 4.3 multiply_subtract_fusion
  (67 shorter events, 17.8 us)
Async XLA Ops:
  7.2 191.5 %all-gather.4.cloned.1.call-start = ((), (), s32[]{:S(2)}) async-start(), calls=%async_computation | async-start | bytes 16920576 | tf_op jit(solution)/shard_map/all_gather | solution.py:130
  8.2 1.8 collective-permute-start
  12.2 191.2 %copy-start.4 = (f32[1152,144]{0,1:T(8,128)S(1)}, f32[1152,144]{0,1:T(8,128)}, u32[]{:S(2)}) copy-start(f32[1152,144]{0,1:T(8,128)} %param.8) | copy-start | bytes 1990660
  12.2 336.6 %all-gather.6.cloned.1.call-start = ((), (), s32[]{:S(2)}) async-start(), calls=%async_computation.1 | async-start | bytes 11280384 | tf_op jit(solution)/shard_map/all_gather | solution.py:152
  201.2 2.2 collective-permute-start.1
  207.1 2.2 collective-permute-start.2
  216.8 283.6 %all-gather.8.cloned.1.call-start = ((), (), s32[]{:S(2)}) async-start(), calls=%async_computation.2 | async-start | bytes 11280384 | tf_op jit(solution)/shard_map/all_gather | solution.py:106
  217.1 1.7 collective-permute-start.3
  218.8 13.8 %slice-start = ((s8[15925248]{0:T(1024)(128)(4,1)}), s8[4194304]{0:T(1024)(128)(4,1)S(1)}, s32[]{:S(2)}) async-start(s8[15925248]{0:T(1024)(128)(4,1)} %bitcast.63), calls=%async_computation.3 | async-start | bytes 8388608
  218.9 13.8 %slice-start.1 = ((s8[15925248]{0:T(1024)(128)(4,1)}), s8[4194304]{0:T(1024)(128)(4,1)S(1)}, s32[]{:S(2)}) async-start(s8[15925248]{0:T(1024)(128)(4,1)} %bitcast.63), calls=%async_computation.4 | async-start | bytes 8388608
  222.6 10.1 %slice-start.2 = ((s8[15925248]{0:T(1024)(128)(4,1)}), s8[4194304]{0:T(1024)(128)(4,1)S(1)}, s32[]{:S(2)}) async-start(s8[15925248]{0:T(1024)(128)(4,1)} %bitcast.63), calls=%async_computation.5 | async-start | bytes 8388608
  227.6 7.1 %copy-start.7 = (f32[1152,144]{0,1:T(8,128)}, f32[1152,144]{0,1:T(8,128)S(1)}, u32[]{:S(2)}) copy-start(f32[1152,144]{0,1:T(8,128)S(1)} %get-tuple-element.21) | copy-start | bytes 1990660
  227.6 7.1 %copy-start.8 = (f32[1152,144]{0,1:T(8,128)}, f32[1152,144]{0,1:T(8,128)S(1)}, u32[]{:S(2)}) copy-start(f32[1152,144]{0,1:T(8,128)S(1)} %get-tuple-element.22) | copy-start | bytes 1990660
  227.6 5.1 slice-start.3
  236.8 20.3 %collective-permute-start.4 = (f32[1152,144]{0,1:T(8,128)S(1)}, f32[1152,144]{0,1:T(8,128)S(1)}, u32[]{:S(2)}, u32[]{:S(2)}) collective-permute-start(f32[1152,144]{0,1:T(8,128)S(1)} %constant_dynamic-slice_fusion), channel_id=1, source_target_pairs={{0,16},{16,0},{1,17},{17,1},{2,18},{18,2},{3,19},{19,3},{4,20},{20... | collective-permute-start | bytes 1990664 | tf_op jit(solution)/shard_map/ppermute | solution.py:59
  238.4 3.7 collective-permute-start.5
  242.8 4.6 collective-permute-start.6
  248.0 3.7 collective-permute-start.7
  251.7 3.7 collective-permute-start.8
  255.4 1.2 collective-permute-start.9
  357.2 3.1 collective-permute-start.10
  368.6 143.6 %copy-start.2 = (f32[1152,144]{0,1:T(8,128)S(1)}, f32[1152,144]{0,1:T(8,128)}, u32[]{:S(2)}) copy-start(f32[1152,144]{0,1:T(8,128)} %fusion.29) | copy-start | bytes 1990660
  500.4 11.8 %copy-start = (f32[1152,2304]{0,1:T(8,128)S(1)}, f32[1152,2304]{0,1:T(8,128)}, u32[]{:S(2)}) copy-start(f32[1152,2304]{0,1:T(8,128)} %all-gather.8.cloned.1.call-done) | copy-start | bytes 31850500
  509.1 3.1 collective-permute-start.11
  (4 other events, 12.3 us)
Sparse Core Ops, SparseCore 0:
  12.3 186.2 all-gather.3
  217.0 131.8 all-gather.5
  368.8 131.6 all-gather.7
where the time goes:
time: 524 us; the launch traced here: 523 us
  waiting for transfers between devices  432 us (82%)
  matrix products  57.4 us (11%)
  between operations  14.8 us (3%)
  other arithmetic  7.58 us (1%)
  starting transfers between devices  6.04 us (1%)
    all_gather x1, waiting for transfers between devices, shards(): lax.all_gather(jnp.stack([grad, basis_hi, basis_lo]), TS, axis=2, tiled=T...  186 us
    all_gather x1, waiting for transfers between devices, newton_step(): iterate_rows = lax.all_gather(iterate, TS, axis=1, tiled=True)  132 us
    all_gather x1, waiting for transfers between devices, shards(): power_rows = lax.all_gather(power, TS, axis=1, tiled=True)  90.8 us
    dot_general x6, matrix products, bf16_dot(): lax.dot_general(left, right, (dims, ((), ())), preferred_element_type=jnp...  24.1 us
    dot_general x2, matrix products, contract_rows(): lax.dot_general(left, right, (((0,), (0,)), ((), ())), precision=lax.Prec...  17.1 us
    dot_general x2, matrix products, exact_dot(): jnp.dot(left, right, precision=lax.Precision.HIGH, preferred_element_type...  12.6 us
    ppermute x8, waiting for transfers between devices, partner(): return lax.ppermute(x, 'shard', [(0, 1), (1, 0)])  12.2 us
    ppermute x4, waiting for transfers between devices, all_sum(): x = x + lax.ppermute(x, TS, [(i, i ^ step) for i in range(n_ts)])  11.2 us
  transfers between devices with their start and end apart: 15, of which 14 were waited for; matrix products, arithmetic and copies ran while one was open for 4% of the time, Pallas kernels for 0%

commit v1 on v0

--- a/solution.py
+++ b/solution.py
@@ -15,6 +15,18 @@
 norm_eps = 1e-06
 TS = ("tensor", "section")
 PAD = 8
+
+
+def doubled_up(x, axis, dim):
+    ways, here = (lax.axis_size(axis), lax.axis_index(axis))
+    grown, reach = (x, 1)
+    while reach < ways:
+        theirs = lax.ppermute(grown, axis, [(d, d ^ reach) for d in range(ways)])
+        mine_first = jnp.concatenate([grown, theirs], axis=dim)
+        theirs_first = jnp.concatenate([theirs, grown], axis=dim)
+        grown = jnp.where(here & reach == 0, mine_first, theirs_first)
+        reach = 2 * reach
+    return grown
 
 
 def exact_dot(left, right):
@@ -103,7 +115,7 @@
         return shard_sum(x)[0, 0]
 
     def newton_step(iterate):
-        iterate_rows = lax.all_gather(iterate, TS, axis=1, tiled=True)
+        iterate_rows = doubled_up(iterate, TS, 1)
         z_cols = shard_sum(contract_rows(iterate_rows, iterate))
         return 1.5 * iterate - 0.5 * exact_dot(iterate_rows, z_cols)
 

time: 524 us -> 661 us (1.26)
  waiting for transfers between devices: 432 us -> 549 us
  other arithmetic: 7.58 us -> 16 us
  matrix products: 57.4 us -> 65.6 us
    ppermute x0 -> x4, waiting for transfers between devices: none -> 248 us  [doubled_up(): theirs = lax.ppermute(grown, axis, [(d, d ^ reach) for d in range(ways)])]
    all_gather x1 -> x0, waiting for transfers between devices: 132 us -> none  [newton_step(): iterate_rows = lax.all_gather(iterate, TS, axis=1, tiled=True)]
    select_n x0 -> x3, other arithmetic: none -> 8.3 us  [doubled_up(): grown = jnp.where(here & reach == 0, mine_first, theirs_first)]
    dot_general x2, matrix products: 12.6 us -> 19.3 us  [exact_dot(): jnp.dot(left, right, precision=lax.Precision.HIGH, preferred_element_type...]
  transfers between devices with their start and end apart: 15 -> 18, of which waited for: 14 -> 17; matrix products, arithmetic and copies ran while one was open for 4% -> 4% of each run, Pallas kernels for 0% -> 0%
where the time goes in v1:
time: 661 us
  waiting for transfers between devices  549 us (83%)
  matrix products  65.6 us (10%)
  other arithmetic  16 us (2%)
  between operations  15.2 us (2%)
  starting transfers between devices  10.3 us (2%)
    ppermute x4, waiting for transfers between devices, doubled_up(): theirs = lax.ppermute(grown, axis, [(d, d ^ reach) for d in range(ways)])  248 us
    all_gather x1, waiting for transfers between devices, shards(): lax.all_gather(jnp.stack([grad, basis_hi, basis_lo]), TS, axis=2, tiled=T...  186 us
    all_gather x1, waiting for transfers between devices, shards(): power_rows = lax.all_gather(power, TS, axis=1, tiled=True)  90.9 us
    dot_general x6, matrix products, bf16_dot(): lax.dot_general(left, right, (dims, ((), ())), preferred_element_type=jnp...  24.2 us
    dot_general x2, matrix products, exact_dot(): jnp.dot(left, right, precision=lax.Precision.HIGH, preferred_element_type...  19.3 us
    dot_general x2, matrix products, contract_rows(): lax.dot_general(left, right, (((0,), (0,)), ((), ())), precision=lax.Prec...  18.4 us
  transfers between devices with their start and end apart: 18, of which 17 were waited for; matrix products, arithmetic and copies ran while one was open for 4% of the time, Pallas kernels for 0%

profile of v1, /device:TPU:0, one launch (start us, length us, event | category | flops | bytes accessed | tf_op | source)
XLA Modules:
  0.0 660.6 jit_solution(4364683551532801337)
XLA Ops:
  12.3 186.3 %all-gather.3.cloned.1.call-done = bf16[3,1152,2304]{1,2,0:T(8,128)(2,1)} async-done(((bf16[3,1152,144]{1,2,0:T(8,128)(2,1)}), bf16[3,1152,2304]{1,2,0:T(8,128)(2,1)}) %all-gather.3.cloned.1.call-update) | async-done | bytes 15925264 | tf_op jit(solution)/shard_map/all_gather | solution.py:142
  201.3 2.1 collective-permute-done.1
  203.4 3.6 fusion.32
  209.6 6.6 fusion
  218.9 3.7 fusion.7
  222.6 5.0 multiply_add_fusion
  227.7 5.0 fusion.9
  238.5 3.6 collective-permute-done.5
  244.1 3.2 collective-permute-done.6
  249.4 2.3 collective-permute-done.7
  253.1 2.3 collective-permute-done.8
  258.1 90.9 %all-gather.5.cloned.1.call-done = f32[1152,2304]{0,1:T(8,128)} async-done(((f32[1152,144]{0,1:T(8,128)}), f32[1152,2304]{0,1:T(8,128)}) %all-gather.5.cloned.1.call-update) | async-done | bytes 10616848 | tf_op jit(solution)/shard_map/all_gather | solution.py:164
  349.0 8.4 %fusion.60 = f32[2304,144]{0,1:T(8,128)S(1)} fusion(f32[1152,2304]{0,1:T(8,128)} %all-gather.5.cloned.1.call-done, f32[1152,144]{0,1:T(8,128)S(1)} %copy-done), kind=kOutput, calls=%fused_computation.84 | convolution fusion | flops 2293235712 | bytes 12607488 | tf_op jit(solution)/shard_map/dot_general | solution.py:37
  358.2 2.5 collective-permute-done.10
  360.7 7.7 %fusion.34 = f32[1152,144]{0,1:T(8,128)S(1)} fusion(f32[1152,2304]{0,1:T(8,128)} %all-gather.5.cloned.1.call-done, f32[2304,144]{0,1:T(8,128)S(1)} %fusion.60, f32[2304,144]{0,1:T(8,128)} %collective-permute-done.10, f32[1152,144]{0,1:T(8,128)S(1)} %copy-done, f32[]{:T(128)S(6)} %mul.109, f32[]{:T(128)S(6)} %mul.104), kind=kOutput, calls=%fused_computation.33 | convolution fusion | flops 2294065152 | bytes 14598152 | tf_op jit(solution)/shard_map/dot_general | solution.py:33
  368.5 16.9 %collective-permute-done.11 = f32[1152,144]{0,1:T(8,128)S(1)} collective-permute-done((f32[1152,144]{0,1:T(8,128)S(1)}, f32[1152,144]{0,1:T(8,128)S(1)}, u32[]{:S(2)}, u32[]{:S(2)}) %collective-permute-start.11) | collective-permute-done | bytes 663584 | tf_op jit(solution)/shard_map/ppermute | solution.py:24
  387.1 58.3 %collective-permute-done.12 = f32[1152,288]{0,1:T(8,128)} collective-permute-done((f32[1152,288]{0,1:T(8,128)S(1)}, f32[1152,288]{0,1:T(8,128)}, u32[]{:S(2)}, u32[]{:S(2)}) %collective-permute-start.12) | collective-permute-done | bytes 1327136 | tf_op jit(solution)/shard_map/ppermute | solution.py:24
  445.4 2.8 maximum_select_fusion.4
  449.7 58.1 %collective-permute-done.13 = f32[1152,576]{0,1:T(8,128)} collective-permute-done((f32[1152,576]{0,1:T(8,128)S(1)}, f32[1152,576]{0,1:T(8,128)}, u32[]{:S(2)}, u32[]{:S(2)}) %collective-permute-start.13) | collective-permute-done | bytes 2654240 | tf_op jit(solution)/shard_map/ppermute | solution.py:24
  507.8 5.4 maximum_select_fusion.3
  514.7 114.3 %collective-permute-done.14 = f32[1152,1152]{0,1:T(8,128)} collective-permute-done((f32[1152,1152]{0,1:T(8,128)}, f32[1152,1152]{0,1:T(8,128)}, u32[]{:S(2)}, u32[]{:S(2)}) %collective-permute-start.14) | collective-permute-done | bytes 5308448 | tf_op jit(solution)/shard_map/ppermute | solution.py:24
  629.0 10.0 %fusion.3 = f32[2304,144]{0,1:T(8,128)S(1)} fusion(f32[1152,144]{0,1:T(8,128)S(1)} %fusion.34, f32[1152,1152]{0,1:T(8,128)} %collective-permute-done.14, f32[1152,1152]{0,1:T(8,128)} %maximum_select_fusion.3, pred[]{:T(512)S(6)} %eq.25), kind=kOutput, calls=%fused_computation.4 | convolution fusion | flops 2301198336 | bytes 12607489 | tf_op jit(solution)/shard_map/dot_general | solution.py:37
  639.1 3.0 collective-permute-done.15
  642.1 11.6 %multiply_subtract_fusion = f32[1152,144]{0,1:T(8,128)} fusion(f32[1152,144]{0,1:T(8,128)S(1)} %fusion.34, f32[2304,144]{0,1:T(8,128)S(1)} %fusion.3, f32[2304,144]{0,1:T(8,128)S(1)} %collective-permute-done.15, f32[1152,1152]{0,1:T(8,128)} %collective-permute-done.14, f32[1152,1152]{0,1:T(8,128)} %maximum_select_fusion.3, pred[]{:T(512)S(6)} %eq.25), kind=kOutput, calls=%fused_computation.59 | convolution fusion | flops 2302027776 | bytes 14598145 | tf_op jit(solution)/shard_map/dot_general | solution.py:33
  (73 shorter events, 31.7 us)
Async XLA Ops:
  7.2 191.5 %all-gather.3.cloned.1.call-start = ((), (), s32[]{:S(2)}) async-start(), calls=%async_computation | async-start | bytes 16920576 | tf_op jit(solution)/shard_map/all_gather | solution.py:142
  8.2 1.8 collective-permute-start
  12.2 191.2 %copy-start.3 = (f32[1152,144]{0,1:T(8,128)S(1)}, f32[1152,144]{0,1:T(8,128)}, u32[]{:S(2)}) copy-start(f32[1152,144]{0,1:T(8,128)} %param.8) | copy-start | bytes 1990660
  12.2 336.8 %all-gather.5.cloned.1.call-start = ((), (), s32[]{:S(2)}) async-start(), calls=%async_computation.1 | async-start | bytes 11280384 | tf_op jit(solution)/shard_map/all_gather | solution.py:164
  201.2 2.2 collective-permute-start.1
  207.1 2.2 collective-permute-start.2
  217.1 1.7 collective-permute-start.3
  218.9 13.8 %slice-start = ((s8[15925248]{0:T(1024)(128)(4,1)}), s8[4194304]{0:T(1024)(128)(4,1)S(1)}, s32[]{:S(2)}) async-start(s8[15925248]{0:T(1024)(128)(4,1)} %bitcast.61), calls=%async_computation.2 | async-start | bytes 8388608
  218.9 13.8 %slice-start.1 = ((s8[15925248]{0:T(1024)(128)(4,1)}), s8[4194304]{0:T(1024)(128)(4,1)S(1)}, s32[]{:S(2)}) async-start(s8[15925248]{0:T(1024)(128)(4,1)} %bitcast.61), calls=%async_computation.3 | async-start | bytes 8388608
  222.6 10.1 %slice-start.2 = ((s8[15925248]{0:T(1024)(128)(4,1)}), s8[4194304]{0:T(1024)(128)(4,1)S(1)}, s32[]{:S(2)}) async-start(s8[15925248]{0:T(1024)(128)(4,1)} %bitcast.61), calls=%async_computation.4 | async-start | bytes 8388608
  227.6 7.1 %copy-start.6 = (f32[1152,144]{0,1:T(8,128)}, f32[1152,144]{0,1:T(8,128)S(1)}, u32[]{:S(2)}) copy-start(f32[1152,144]{0,1:T(8,128)S(1)} %get-tuple-element.21) | copy-start | bytes 1990660
  227.6 7.1 %copy-start.7 = (f32[1152,144]{0,1:T(8,128)}, f32[1152,144]{0,1:T(8,128)S(1)}, u32[]{:S(2)}) copy-start(f32[1152,144]{0,1:T(8,128)S(1)} %get-tuple-element.22) | copy-start | bytes 1990660
  236.8 20.4 %collective-permute-start.4 = (f32[1152,144]{0,1:T(8,128)S(1)}, f32[1152,144]{0,1:T(8,128)S(1)}, u32[]{:S(2)}, u32[]{:S(2)}) collective-permute-start(f32[1152,144]{0,1:T(8,128)S(1)} %constant_dynamic-slice_fusion), channel_id=1, source_target_pairs={{0,16},{16,0},{1,17},{17,1},{2,18},{18,2},{3,19},{19,3},{4,20},{20... | collective-permute-start | bytes 1990664 | tf_op jit(solution)/shard_map/ppermute | solution.py:71
  238.4 3.7 collective-permute-start.5
  242.8 4.6 collective-permute-start.6
  248.0 3.7 collective-permute-start.7
  251.7 3.7 collective-permute-start.8
  255.4 1.2 collective-permute-start.9
  357.4 3.3 collective-permute-start.10
  368.4 17.0 %collective-permute-start.11 = (f32[1152,144]{0,1:T(8,128)S(1)}, f32[1152,144]{0,1:T(8,128)S(1)}, u32[]{:S(2)}, u32[]{:S(2)}) collective-permute-start(f32[1152,144]{0,1:T(8,128)S(1)} %fusion.34), channel_id=1, source_target_pairs={{0,1},{1,0},{2,3},{3,2},{4,5},{5,4},{6,7},{7,6},{8,9},{9,8},{10,11... | collective-permute-start | bytes 1990664 | tf_op jit(solution)/shard_map/ppermute | solution.py:24
  385.5 59.9 %collective-permute-start.12 = (f32[1152,288]{0,1:T(8,128)S(1)}, f32[1152,288]{0,1:T(8,128)}, u32[]{:S(2)}, u32[]{:S(2)}) collective-permute-start(f32[1152,288]{0,1:T(8,128)S(1)} %maximum_select_fusion.7), channel_id=1, source_target_pairs={{0,2},{1,3},{2,0},{3,1},{4,6},{5,7},{6,4},{7,5},{8,10},{9,11},{10,... | collective-permute-start | bytes 3981320 | tf_op jit(solution)/shard_map/ppermute | solution.py:24
  448.2 59.6 %collective-permute-start.13 = (f32[1152,576]{0,1:T(8,128)S(1)}, f32[1152,576]{0,1:T(8,128)}, u32[]{:S(2)}, u32[]{:S(2)}) collective-permute-start(f32[1152,576]{0,1:T(8,128)S(1)} %maximum_select_fusion.4), channel_id=1, source_target_pairs={{0,4},{1,5},{2,6},{3,7},{4,0},{5,1},{6,2},{7,3},{8,12},{9,13},{10,... | collective-permute-start | bytes 7962632 | tf_op jit(solution)/shard_map/ppermute | solution.py:24
  513.2 115.8 %collective-permute-start.14 = (f32[1152,1152]{0,1:T(8,128)}, f32[1152,1152]{0,1:T(8,128)}, u32[]{:S(2)}, u32[]{:S(2)}) collective-permute-start(f32[1152,1152]{0,1:T(8,128)} %maximum_select_fusion.3), channel_id=1, source_target_pairs={{0,8},{1,9},{2,10},{3,11},{4,12},{5,13},{6,14},{7,15},{8,0},{9,1},... | collective-permute-start | bytes 15925256 | tf_op jit(solution)/shard_map/ppermute | solution.py:24
  639.0 3.1 collective-permute-start.15
  (6 other events, 19.1 us)
Sparse Core Ops, SparseCore 0:
  12.3 186.2 all-gather.2
  217.2 131.7 all-gather.4
